TPU v7x, 512 devices: a whole 4x8x8 slice. The times are simulated.
512 devices in a mesh: blk: 64 (over x, z, y_hi), dp: 8 (over y_lo, core).
Axes of the slice: x: 4, y: 8 (y_hi: 2, y_lo: 4; y = y_hi * 4 + y_lo), z: 8, core: 2. Of those that a mesh axis runs over, the one named last changes fastest.
Arguments:
- input_field: bfloat16 [262144, 2048], P('blk', 'dp'), may hold values from -6 to 6
- target_field: bfloat16 [262144, 2048], P('blk', 'dp'), may hold values from -6 to 6
- first_factor: bfloat16 [256, 1024, 256], P('dp', 'blk'), may hold values from -0.375 to 0.375
- second_factor: bfloat16 [256, 1024, 256], P('dp', 'blk'), may hold values from -0.375 to 0.375
Outputs:
- first_grad: bfloat16 [256, 1024, 256], P('dp', 'blk')
- second_grad: bfloat16 [256, 1024, 256], P('dp', 'blk')
All inputs are finite; a program needn't handle non-finite values.
Results may differ from a plain program's by a relative error of at most 0.012.
Values may be sent and summed in bfloat16 or wider, within the bound.
No kernel may reach another device: no remote copies, remote signals or barrier semaphores. Data moves between devices by JAX's collectives and lax.ppermute only.
A program may use at most 64 MiB of HBM per device.

v0:
```python
import math
import jax
import jax.numpy as jnp
from jax import lax
from jax.experimental.layout import Layout, with_layout_constraint
from jax.sharding import Mesh
from jax.sharding import PartitionSpec as P

NB = 1024
BS = 256
tanh_scale = 0.7978845608028654
cubic_coef = 0.044715


def gelu_value(values):
    inner = jnp.tanh(tanh_scale * (values + cubic_coef * values * values * values))
    return 0.5 * values * (1.0 + inner)


def gelu_slope(values):
    inner = jnp.tanh(tanh_scale * (values + cubic_coef * values * values * values))
    return 0.5 * (1.0 + inner) + 0.5 * values * (1.0 - inner * inner) * tanh_scale * (
        1.0 + 3.0 * cubic_coef * values * values
    )


def line_pairs(n, step):
    return [(i, i + step) for i in range(n) if 0 <= i + step < n]


def swap_pairs(n):
    return [(c, (c + 1) % n) for c in range(n)]


def swap_pairs(n):
    return [(c, (c + 1) % n) for c in range(n)]


def gather_rows(piece):
    n_core = lax.axis_size("core")
    n_ylo = lax.axis_size("ylo")
    c = lax.axis_index("core")
    copies = jnp.broadcast_to(piece[None], (n_ylo,) + piece.shape)
    line = lax.all_to_all(copies, "ylo", split_axis=0, concat_axis=0, tiled=True)
    other = lax.ppermute(line, "core", swap_pairs(n_core))
    pair = jnp.zeros((n_ylo, n_core) + piece.shape, piece.dtype)
    pair = lax.dynamic_update_index_in_dim(pair, line, c, 1)
    pair = lax.dynamic_update_index_in_dim(pair, other, lax.rem(c + 1, n_core), 1)
    return pair.reshape((n_ylo * n_core * piece.shape[0],) + piece.shape[1:])


def scatter_rows(term):
    n_core = lax.axis_size("core")
    n_ylo = lax.axis_size("ylo")
    c = lax.axis_index("core")
    blocks, total_rows, width = term.shape
    rows = total_rows // (n_core * n_ylo)
    split = term.reshape(blocks, n_ylo, n_core, rows, width)
    sent = lax.dynamic_index_in_dim(split, lax.rem(c + 1, n_core), 2, keepdims=False)
    kept = lax.dynamic_index_in_dim(split, c, 2, keepdims=False)
    got = lax.ppermute(sent, "core", swap_pairs(n_core))
    half = (kept.astype(jnp.float32) + got.astype(jnp.float32)).astype(jnp.bfloat16)
    arrived = lax.all_to_all(half, "ylo", split_axis=1, concat_axis=1, tiled=True)
    total = jnp.sum(arrived.astype(jnp.float32), axis=1).astype(jnp.bfloat16)
    return jnp.transpose(total, (1, 0, 2))


def shards(input_field, target_field, first_factor, second_factor):
    block_count = first_factor.shape[1]
    block_size = first_factor.shape[2]
    row_count = input_field.shape[1]
    dp = ("ylo", "core")
    replica_count = lax.axis_size("ylo") * lax.axis_size("core")
    blk_count = lax.axis_size("blk")
    group_count = NB // BS
    inner_count = block_count // group_count
    scale_factor = 1.0 / math.sqrt(row_count * replica_count)
    inputs = input_field.reshape(block_count, block_size, row_count)
    first_full = gather_rows(first_factor)
    second_full = lax.all_gather(second_factor, dp, axis=0, tiled=True)
    pre_act = jnp.einsum("bkr,kbi->bir", inputs, first_full, preferred_element_type=jnp.float32)
    pre_split = pre_act.reshape(block_count, blk_count, inner_count, row_count)
    activated = gelu_value(pre_split).astype(jnp.bfloat16)
    slope = jnp.transpose(gelu_slope(pre_split).astype(jnp.bfloat16), (2, 1, 0, 3))
    activated, second_full, slope = lax.optimization_barrier((activated, second_full, slope))
    sending = jnp.transpose(activated, (2, 1, 0, 3))
    sending = with_layout_constraint(sending, Layout((1, 0, 2, 3)))
    received = lax.all_to_all(sending, "blk", split_axis=1, concat_axis=1, tiled=True)
    permuted = received.reshape(block_count, block_size, row_count)
    targets = target_field.reshape(block_count, block_size, row_count)
    second_t = jnp.transpose(second_full, (1, 0, 2))
    predicted = jnp.einsum("qcj,qcr->qjr", second_t, permuted, preferred_element_type=jnp.float32)
    residual = ((predicted - targets.astype(jnp.float32)) * scale_factor).astype(jnp.bfloat16)
    permuted_grad = jnp.einsum(
        "qcj,qjr->qcr", second_t, residual, preferred_element_type=jnp.float32
    ).astype(jnp.bfloat16)
    term = jnp.einsum("qcr,qjr->cqj", permuted, residual, preferred_element_type=jnp.float32)
    second_out = lax.psum_scatter(term.astype(jnp.bfloat16), dp, scatter_dimension=0, tiled=True)
    back = permuted_grad.reshape(inner_count, blk_count, block_count, row_count)
    back = with_layout_constraint(back, Layout((1, 0, 2, 3)))
    activated_grad = lax.all_to_all(back, "blk", split_axis=1, concat_axis=1, tiled=True)
    pre_grad = (activated_grad.astype(jnp.float32) * slope).astype(jnp.bfloat16)
    pre_grad = jnp.transpose(pre_grad, (2, 1, 0, 3)).reshape(block_count, block_size, row_count)
    first_sum = scatter_rows(
        jnp.einsum("bkr,bir->bki", inputs, pre_grad, preferred_element_type=jnp.float32).astype(
            jnp.bfloat16
        )
    )
    return (first_sum, second_out)


def solution(mesh):
    n_blk, n_dp = mesh.devices.shape
    n_core = 2
    split_mesh = Mesh(mesh.devices.reshape(n_blk, n_dp // n_core, n_core), ("blk", "ylo", "core"))
    dp = ("ylo", "core")
    return jax.shard_map(
        shards,
        mesh=split_mesh,
        in_specs=(P("blk", dp), P("blk", dp), P(dp, "blk", None), P(dp, "blk", None)),
        out_specs=(P(dp, "blk", None), P(dp, "blk", None)),
        check_vma=False,
    )
```

profile of v0, /device:TPU:1, one launch (start us, length us, event | category | flops | bytes accessed | tf_op | source)
XLA Modules:
  0.0 266.5 jit_solution(7686284974705807812)
XLA Ops:
  7.2 0.0 copy-start
  7.2 2.2 broadcast_in_dim.17
  9.3 5.4 %all-to-all-start = ((bf16[4,32,16,256]{3,2,1,0:T(8,128)(2,1)}), bf16[4,32,16,256]{3,2,1,0:T(8,128)(2,1)S(1)}, u32[]{:S(2)}, u32[]{:S(2)}) async-start(bf16[4,32,16,256]{3,2,1,0:T(8,128)(2,1)} %broadcast_in_dim.17), calls=%async_computation | async-start | bytes 2097152 | tf_op jit(solution)/shard_map/all_to_all | solution.py:44
  14.8 0.0 all-gather.2.cloned.1.call-start
  14.8 0.7 all-gather.2.cloned.1.call-update
  15.5 22.9 %all-to-all-done = bf16[4,32,16,256]{3,2,1,0:T(8,128)(2,1)S(1)} async-done(((bf16[4,32,16,256]{3,2,1,0:T(8,128)(2,1)}), bf16[4,32,16,256]{3,2,1,0:T(8,128)(2,1)S(1)}, u32[]{:S(2)}, u32[]{:S(2)}) %all-to-all-start) | async-done | bytes 1048608 | tf_op jit(solution)/shard_map/all_to_all | solution.py:44
  38.4 9.8 %collective-permute-start = (bf16[4,32,16,256]{3,2,1,0:T(8,128)(2,1)S(1)}, bf16[4,32,16,256]{3,2,1,0:T(8,128)(2,1)}, u32[]{:S(2)}, u32[]{:S(2)}) collective-permute-start(bf16[4,32,16,256]{3,2,1,0:T(8,128)(2,1)S(1)} %all-to-all-done), channel_id=1, source_target_pairs={{0,1},{1,0},{2,3},{3,2},{4,5},{5,4},{6,7},{7,6},{8,9},{9,8},{10,11... | collective-permute-start | bytes 3145736 | tf_op jit(solution)/shard_map/ppermute | solution.py:45
  48.2 0.2 broadcast_in_dim.16
  48.4 0.1 bitcast_dynamic-update-slice_fusion.1
  48.5 2.1 collective-permute-done
  50.6 1.3 bitcast_dynamic-update-slice_fusion
  51.9 0.0 copy-done
  51.9 1.5 fusion.11
  53.5 2.4 copy.26
  55.9 4.2 %fusion.13 = (bf16[4,64,16,256]{3,2,0,1:T(8,128)(2,1)}, bf16[16,64,4,256]{3,0,2,1:T(8,128)(2,1)}) fusion(f32[16,64,4,256]{3,0,2,1:T(8,128)S(1)} %bitcast.46), kind=kLoop, calls=%fused_computation.20 | loop fusion | flops 20971520 | bytes 8388608 | tf_op jit(solution)/shard_map/transpose | solution.py:84
  60.0 1.9 all-gather.2.cloned.1.call-done
  62.0 73.9 %all_to_all.20 = bf16[4,64,16,256]{3,2,0,1:T(8,128)(2,1)S(1)} all-to-all(bf16[4,64,16,256]{3,2,0,1:T(8,128)(2,1)} %bitcast.52), channel_id=1, replica_groups=mesh['blk'=64,'ylo'=4,'core'=2] {'blk'}, dimensions={1} | all-to-all | bytes 4194304 | tf_op jit(solution)/shard_map/all_to_all | solution.py:88
  135.9 0.0 copy-start.3
  135.9 0.0 copy-start.4
  135.9 0.2 copy.27
  136.1 0.0 copy-start.2
  136.1 2.2 copy-done.3
  138.3 0.6 copy-done.4
  138.9 1.7 fusion.7
  140.6 0.0 copy-done.2
  140.6 0.0 copy-start.1
  140.6 0.9 convolution_convert_fusion
  141.5 0.5 copy-done.1
  142.0 1.6 copy.30
  143.6 7.7 %all-to-all-start.2 = ((bf16[4,64,16,256]{3,2,0,1:T(8,128)(2,1)}), bf16[4,64,16,256]{3,2,0,1:T(8,128)(2,1)}, u32[]{:S(2)}, u32[]{:S(2)}) async-start(bf16[4,64,16,256]{3,2,0,1:T(8,128)(2,1)} %copy.30), calls=%async_computation.2 | async-start | bytes 4194304 | tf_op jit(solution)/shard_map/all_to_all | solution.py:101
  151.3 0.2 reduce-scatter.2.cloned.1.call-start
  151.5 4.3 %convert_bitcast_fusion = bf16[256,16,256]{0,2,1:T(8,128)(2,1)} fusion(bf16[16,256,256]{2,1,0:T(8,128)(2,1)} %copy-done.1, bf16[16,256,256]{2,1,0:T(8,128)(2,1)} %bitcast.45), kind=kOutput, calls=%fused_computation.19 | convolution fusion | flops 537919488 | bytes 6291456 | tf_op jit(solution)/shard_map/qcr,qjr->cqj/dot_general | solution.py:97
  155.8 4.6 %copy.35 = bf16[256,16,256]{2,1,0:T(8,128)(2,1)} copy(bf16[256,16,256]{0,2,1:T(8,128)(2,1)} %convert_bitcast_fusion) | data formatting | bytes 4194304 | tf_op jit(solution)/shard_map/convert_element_type | solution.py:98
  160.4 0.0 reduce-scatter.2.cloned.1.call-update
  160.4 51.0 %all-to-all-done.2 = bf16[4,64,16,256]{3,2,0,1:T(8,128)(2,1)} async-done(((bf16[4,64,16,256]{3,2,0,1:T(8,128)(2,1)}), bf16[4,64,16,256]{3,2,0,1:T(8,128)(2,1)}, u32[]{:S(2)}, u32[]{:S(2)}) %all-to-all-start.2) | async-done | bytes 2097184 | tf_op jit(solution)/shard_map/all_to_all | solution.py:101
  211.5 3.2 %multiply_convert_fusion = bf16[4,64,16,256]{3,2,0,1:T(8,128)(2,1)S(1)} fusion(bf16[4,64,16,256]{3,2,0,1:T(8,128)(2,1)} %get-tuple-element.7, bf16[4,64,16,256]{3,2,0,1:T(8,128)(2,1)} %all-to-all-done.2), kind=kLoop, calls=%fused_computation.11 | loop fusion | flops 4194304 | bytes 6291456 | tf_op jit(solution)/shard_map/convert_element_type | solution.py:102
  214.7 1.0 fusion.14
  215.7 0.2 constant_dynamic-slice_fusion.1
  215.9 0.1 copy.53
  215.9 8.3 %collective-permute-start.1 = (bf16[16,4,32,256]{3,2,0,1:T(8,128)(2,1)S(1)}, bf16[16,4,32,256]{3,2,0,1:T(8,128)(2,1)S(1)}, u32[]{:S(2)}, u32[]{:S(2)}) collective-permute-start(bf16[16,4,32,256]{3,2,0,1:T(8,128)(2,1)S(1)} %bitcast.56), channel_id=1, source_target_pairs={{0,1},{1,0},{2,3},{3,2},{4,5},{5,4},{6,7},{7,6},{8,9},{9,8},{10,11... | collective-permute-start | bytes 3145736 | tf_op jit(solution)/shard_map/ppermute | solution.py:61
  224.3 2.3 collective-permute-done.1
  226.5 0.4 fusion.8
  227.0 31.6 %all_to_all.21 = bf16[16,4,32,256]{3,2,0,1:T(8,128)(2,1)S(1)} all-to-all(bf16[16,4,32,256]{3,2,0,1:T(8,128)(2,1)S(1)} %fusion.8), channel_id=1, replica_groups=mesh['blk'=64,'ylo'=4,'core'=2] {'ylo'}, dimensions={1} | all-to-all | bytes 2097152 | tf_op jit(solution)/shard_map/all_to_all | solution.py:63
  258.6 0.2 reduce_sum.12
  258.8 0.9 copy.36
  259.6 0.0 reduce-scatter.2.cloned.1.call-done
Async XLA Ops:
  7.2 44.8 %copy-start = (bf16[4096,256]{1,0:T(8,128)(2,1)S(1)}, bf16[4096,256]{1,0:T(8,128)(2,1)}, u32[]{:S(2)}) copy-start(bf16[4096,256]{1,0:T(8,128)(2,1)} %param.4) | copy-start | bytes 6291460
  9.3 29.0 %all-to-all-start = ((bf16[4,32,16,256]{3,2,1,0:T(8,128)(2,1)}), bf16[4,32,16,256]{3,2,1,0:T(8,128)(2,1)S(1)}, u32[]{:S(2)}, u32[]{:S(2)}) async-start(bf16[4,32,16,256]{3,2,1,0:T(8,128)(2,1)} %broadcast_in_dim.17), calls=%async_computation | async-start | bytes 2097152 | tf_op jit(solution)/shard_map/all_to_all | solution.py:44
  14.8 47.2 %all-gather.2.cloned.1.call-start = ((), (), s32[]{:S(2)}) async-start(), calls=%async_computation.5 | async-start | bytes 2359296 | tf_op jit(solution)/shard_map/all_gather | solution.py:80
  38.4 12.2 %collective-permute-start = (bf16[4,32,16,256]{3,2,1,0:T(8,128)(2,1)S(1)}, bf16[4,32,16,256]{3,2,1,0:T(8,128)(2,1)}, u32[]{:S(2)}, u32[]{:S(2)}) collective-permute-start(bf16[4,32,16,256]{3,2,1,0:T(8,128)(2,1)S(1)} %all-to-all-done), channel_id=1, source_target_pairs={{0,1},{1,0},{2,3},{3,2},{4,5},{5,4},{6,7},{7,6},{8,9},{9,8},{10,11... | collective-permute-start | bytes 3145736 | tf_op jit(solution)/shard_map/ppermute | solution.py:45
  135.9 2.3 copy-start.3
  135.9 3.0 %copy-start.4 = (bf16[4096,256]{1,0:T(8,128)(2,1)S(1)}, bf16[4096,256]{1,0:T(8,128)(2,1)}, u32[]{:S(2)}) copy-start(bf16[4096,256]{1,0:T(8,128)(2,1)} %param.5) | copy-start | bytes 6291460
  136.1 4.5 %copy-start.2 = (bf16[4,64,16,256]{3,2,1,0:T(8,128)(2,1)}, bf16[4,64,16,256]{3,2,1,0:T(8,128)(2,1)S(1)}, u32[]{:S(2)}) copy-start(bf16[4,64,16,256]{3,2,1,0:T(8,128)(2,1)S(1)} %copy.27) | copy-start | bytes 6291460
  140.6 1.4 copy-start.1
  143.6 67.9 %all-to-all-start.2 = ((bf16[4,64,16,256]{3,2,0,1:T(8,128)(2,1)}), bf16[4,64,16,256]{3,2,0,1:T(8,128)(2,1)}, u32[]{:S(2)}, u32[]{:S(2)}) async-start(bf16[4,64,16,256]{3,2,0,1:T(8,128)(2,1)} %copy.30), calls=%async_computation.2 | async-start | bytes 4194304 | tf_op jit(solution)/shard_map/all_to_all | solution.py:101
  151.3 108.4 %reduce-scatter.2.cloned.1.call-start = ((), (), s32[]{:S(2)}) async-start(), calls=%async_computation.6 | async-start | bytes 2359296 | tf_op jit(solution)/shard_map/reduce_scatter | solution.py:98
  215.9 10.6 %collective-permute-start.1 = (bf16[16,4,32,256]{3,2,0,1:T(8,128)(2,1)S(1)}, bf16[16,4,32,256]{3,2,0,1:T(8,128)(2,1)S(1)}, u32[]{:S(2)}, u32[]{:S(2)}) collective-permute-start(bf16[16,4,32,256]{3,2,0,1:T(8,128)(2,1)S(1)} %bitcast.56), channel_id=1, source_target_pairs={{0,1},{1,0},{2,3},{3,2},{4,5},{5,4},{6,7},{7,6},{8,9},{9,8},{10,11... | collective-permute-start | bytes 3145736 | tf_op jit(solution)/shard_map/ppermute | solution.py:61
Sparse Core Ops, SparseCore 0:
  17.7 44.2 all-gather.1
  160.6 60.7 reduce-scatter.1
where the time goes:
time: 267 us; the launch traced here: 266 us
  blocking collectives  106 us (40%)
  waiting for transfers between devices  81 us (30%)
  starting transfers between devices  31.5 us (12%)
  local copies, waits for them, and re-layouts  16.9 us (6%)
  between operations  14.2 us (5%)
  matrix products  9.36 us (4%)
  other arithmetic  7.96 us (3%)
    all_to_all x1, blocking collectives, shards(): lax.all_to_all(sending, 'blk', split_axis=1, concat_axis=1, tiled=True)  73.9 us
    all_to_all x1, waiting for transfers between devices, shards(): lax.all_to_all(back, 'blk', split_axis=1, concat_axis=1, tiled=True)  51 us
    all_to_all x1, blocking collectives, scatter_rows(): lax.all_to_all(half, 'ylo', split_axis=1, concat_axis=1, tiled=True)  31.6 us
    all_to_all x1, waiting for transfers between devices, gather_rows(): lax.all_to_all(copies, 'ylo', split_axis=0, concat_axis=0, tiled=True)  22.9 us
    ppermute x1, starting transfers between devices, gather_rows(): other = lax.ppermute(line, 'core', swap_pairs(n_core))  9.84 us
    ppermute x1, starting transfers between devices, scatter_rows(): got = lax.ppermute(sent, 'core', swap_pairs(n_core))  8.32 us
    all_to_all x1, starting transfers between devices, shards(): lax.all_to_all(back, 'blk', split_axis=1, concat_axis=1, tiled=True)  7.73 us
    all_to_all x1, starting transfers between devices, gather_rows(): lax.all_to_all(copies, 'ylo', split_axis=0, concat_axis=0, tiled=True)  5.42 us
  transfers between devices with their start and end apart: 6, of which 5 were waited for; matrix products, arithmetic and copies ran while one was open for 9% of the time, Pallas kernels for 0%

commit v1 on v0

--- a/solution.py
+++ b/solution.py
@@ -60,7 +60,10 @@
     kept = lax.dynamic_index_in_dim(split, c, 2, keepdims=False)
     got = lax.ppermute(sent, "core", swap_pairs(n_core))
     half = (kept.astype(jnp.float32) + got.astype(jnp.float32)).astype(jnp.bfloat16)
-    arrived = lax.all_to_all(half, "ylo", split_axis=1, concat_axis=1, tiled=True)
+    arrived = jnp.concatenate(
+        lax.all_to_all(jnp.stack(jnp.split(half, lax.axis_size("ylo"), axis=1)), "ylo", 0, 0),
+        axis=1,
+    )
     total = jnp.sum(arrived.astype(jnp.float32), axis=1).astype(jnp.bfloat16)
     return jnp.transpose(total, (1, 0, 2))
 

time: 267 us -> 264 us (0.989)
  waiting for transfers between devices: 81 us -> 78.3 us
    all_to_all x1, waiting for transfers between devices: 51 us -> 48.4 us  [shards(): lax.all_to_all(back, 'blk', split_axis=1, concat_axis=1, tiled=True)]
where the time goes in v1:
time: 264 us
  blocking collectives  104 us (39%)
  waiting for transfers between devices  78.3 us (30%)
  starting transfers between devices  32.8 us (12%)
  local copies, waits for them, and re-layouts  17 us (6%)
  between operations  14.2 us (5%)
  matrix products  9.36 us (4%)
  other arithmetic  8.08 us (3%)
    all_to_all x1, blocking collectives, shards(): lax.all_to_all(sending, 'blk', split_axis=1, concat_axis=1, tiled=True)  73.6 us
    all_to_all x1, waiting for transfers between devices, shards(): lax.all_to_all(back, 'blk', split_axis=1, concat_axis=1, tiled=True)  48.4 us
    all_to_all x1, blocking collectives, scatter_rows(): lax.all_to_all(jnp.stack(jnp.split(half, lax.axis_size('ylo'), axis=1)),...  30.3 us
    all_to_all x1, waiting for transfers between devices, gather_rows(): lax.all_to_all(copies, 'ylo', split_axis=0, concat_axis=0, tiled=True)  22.9 us
    ppermute x1, starting transfers between devices, scatter_rows(): got = lax.ppermute(sent, 'core', swap_pairs(n_core))  9.85 us
    ppermute x1, starting transfers between devices, gather_rows(): other = lax.ppermute(line, 'core', swap_pairs(n_core))  9.84 us
    all_to_all x1, starting transfers between devices, shards(): lax.all_to_all(back, 'blk', split_axis=1, concat_axis=1, tiled=True)  7.42 us
    all_to_all x1, starting transfers between devices, gather_rows(): lax.all_to_all(copies, 'ylo', split_axis=0, concat_axis=0, tiled=True)  5.42 us
  transfers between devices with their start and end apart: 6, of which 5 were waited for; matrix products, arithmetic and copies ran while one was open for 9% of the time, Pallas kernels for 0%

profile of v1, /device:TPU:1, one launch (start us, length us, event | category | flops | bytes accessed | tf_op | source)
XLA Modules:
  0.0 263.6 jit_solution(7122618577009928712)
XLA Ops:
  7.2 0.0 copy-start
  7.2 2.2 broadcast_in_dim.17
  9.3 5.4 %all-to-all-start = ((bf16[4,32,16,256]{3,2,1,0:T(8,128)(2,1)}), bf16[4,32,16,256]{3,2,1,0:T(8,128)(2,1)S(1)}, u32[]{:S(2)}, u32[]{:S(2)}) async-start(bf16[4,32,16,256]{3,2,1,0:T(8,128)(2,1)} %broadcast_in_dim.17), calls=%async_computation | async-start | bytes 2097152 | tf_op jit(solution)/shard_map/all_to_all | solution.py:44
  14.8 0.0 all-gather.2.cloned.1.call-start
  14.8 0.7 all-gather.2.cloned.1.call-update
  15.5 22.9 %all-to-all-done = bf16[4,32,16,256]{3,2,1,0:T(8,128)(2,1)S(1)} async-done(((bf16[4,32,16,256]{3,2,1,0:T(8,128)(2,1)}), bf16[4,32,16,256]{3,2,1,0:T(8,128)(2,1)S(1)}, u32[]{:S(2)}, u32[]{:S(2)}) %all-to-all-start) | async-done | bytes 1048608 | tf_op jit(solution)/shard_map/all_to_all | solution.py:44
  38.4 9.8 %collective-permute-start = (bf16[4,32,16,256]{3,2,1,0:T(8,128)(2,1)S(1)}, bf16[4,32,16,256]{3,2,1,0:T(8,128)(2,1)}, u32[]{:S(2)}, u32[]{:S(2)}) collective-permute-start(bf16[4,32,16,256]{3,2,1,0:T(8,128)(2,1)S(1)} %all-to-all-done), channel_id=1, source_target_pairs={{0,1},{1,0},{2,3},{3,2},{4,5},{5,4},{6,7},{7,6},{8,9},{9,8},{10,11... | collective-permute-start | bytes 3145736 | tf_op jit(solution)/shard_map/ppermute | solution.py:45
  48.2 0.2 broadcast_in_dim.16
  48.4 0.1 bitcast_dynamic-update-slice_fusion.1
  48.5 2.1 collective-permute-done
  50.6 1.3 bitcast_dynamic-update-slice_fusion
  51.9 0.0 copy-done
  52.0 1.5 fusion.11
  53.5 2.4 copy.32
  55.9 4.1 %fusion.13 = (bf16[4,64,16,256]{3,2,0,1:T(8,128)(2,1)}, bf16[16,64,4,256]{3,0,2,1:T(8,128)(2,1)}) fusion(f32[16,64,4,256]{3,0,2,1:T(8,128)S(1)} %bitcast.54), kind=kLoop, calls=%fused_computation.20 | loop fusion | flops 20971520 | bytes 8388608 | tf_op jit(solution)/shard_map/transpose | solution.py:87
  60.1 1.9 all-gather.2.cloned.1.call-done
  62.0 73.6 %all_to_all.20 = bf16[4,64,16,256]{3,2,0,1:T(8,128)(2,1)S(1)} all-to-all(bf16[4,64,16,256]{3,2,0,1:T(8,128)(2,1)} %bitcast.60), channel_id=1, replica_groups=mesh['blk'=64,'ylo'=4,'core'=2] {'blk'}, dimensions={1} | all-to-all | bytes 4194304 | tf_op jit(solution)/shard_map/all_to_all | solution.py:91
  135.6 0.0 copy-start.3
  135.6 0.0 copy-start.4
  135.6 0.2 copy.33
  135.7 0.0 copy-start.2
  135.7 2.2 copy-done.3
  137.9 0.6 copy-done.4
  138.5 1.7 fusion.7
  140.2 0.0 copy-done.2
  140.3 0.0 copy-start.1
  140.3 0.9 convolution_convert_fusion
  141.1 0.5 copy-done.1
  141.6 1.6 copy.36
  143.2 7.4 %all-to-all-start.2 = ((bf16[4,64,16,256]{3,2,0,1:T(8,128)(2,1)}), bf16[4,64,16,256]{3,2,0,1:T(8,128)(2,1)}, u32[]{:S(2)}, u32[]{:S(2)}) async-start(bf16[4,64,16,256]{3,2,0,1:T(8,128)(2,1)} %copy.36), calls=%async_computation.2 | async-start | bytes 4194304 | tf_op jit(solution)/shard_map/all_to_all | solution.py:104
  150.7 0.2 reduce-scatter.2.cloned.1.call-start
  150.9 4.3 %convert_bitcast_fusion = bf16[256,16,256]{0,2,1:T(8,128)(2,1)} fusion(bf16[16,256,256]{2,1,0:T(8,128)(2,1)} %copy-done.1, bf16[16,256,256]{2,1,0:T(8,128)(2,1)} %bitcast.53), kind=kOutput, calls=%fused_computation.19 | convolution fusion | flops 537919488 | bytes 6291456 | tf_op jit(solution)/shard_map/qcr,qjr->cqj/dot_general | solution.py:100
  155.2 4.6 %copy.40 = bf16[256,16,256]{2,1,0:T(8,128)(2,1)} copy(bf16[256,16,256]{0,2,1:T(8,128)(2,1)} %convert_bitcast_fusion) | data formatting | bytes 4194304 | tf_op jit(solution)/shard_map/convert_element_type | solution.py:101
  159.8 0.0 reduce-scatter.2.cloned.1.call-update
  159.8 48.4 %all-to-all-done.2 = bf16[4,64,16,256]{3,2,0,1:T(8,128)(2,1)} async-done(((bf16[4,64,16,256]{3,2,0,1:T(8,128)(2,1)}), bf16[4,64,16,256]{3,2,0,1:T(8,128)(2,1)}, u32[]{:S(2)}, u32[]{:S(2)}) %all-to-all-start.2) | async-done | bytes 2097184 | tf_op jit(solution)/shard_map/all_to_all | solution.py:104
  208.1 3.2 %multiply_convert_fusion = bf16[4,64,16,256]{3,2,0,1:T(8,128)(2,1)S(1)} fusion(bf16[4,64,16,256]{3,2,0,1:T(8,128)(2,1)} %get-tuple-element.7, bf16[4,64,16,256]{3,2,0,1:T(8,128)(2,1)} %all-to-all-done.2), kind=kLoop, calls=%fused_computation.11 | loop fusion | flops 4194304 | bytes 6291456 | tf_op jit(solution)/shard_map/convert_element_type | solution.py:105
  211.3 1.0 fusion.14
  212.3 0.2 constant_dynamic-slice_fusion.1
  212.5 0.1 copy.57
  212.6 9.8 %collective-permute-start.1 = (bf16[16,4,32,256]{3,2,0,1:T(8,128)(2,1)S(1)}, bf16[16,4,32,256]{3,2,0,1:T(8,128)(2,1)S(1)}, u32[]{:S(2)}, u32[]{:S(2)}) collective-permute-start(bf16[16,4,32,256]{3,2,0,1:T(8,128)(2,1)S(1)} %bitcast.64), channel_id=1, source_target_pairs={{0,1},{1,0},{2,3},{3,2},{4,5},{5,4},{6,7},{7,6},{8,9},{9,8},{10,11... | collective-permute-start | bytes 3145736 | tf_op jit(solution)/shard_map/ppermute | solution.py:61
  222.4 2.3 collective-permute-done.1
  224.7 0.4 fusion.8
  225.2 0.1 slice_bitcast_fusion.3
  225.2 0.1 pad_maximum_fusion
  225.4 30.3 %all_to_all.21 = bf16[4,16,1,32,256]{4,3,1,2,0:T(8,128)(2,1)S(1)} all-to-all(bf16[4,16,1,32,256]{4,3,1,2,0:T(8,128)(2,1)S(1)} %pad_maximum_fusion), channel_id=1, replica_groups=mesh['blk'=64,'ylo'=4,'core'=2] {'ylo'}, dimensions={0} | all-to-all | bytes 2097152 | tf_op jit(solution)/shard_map/all_to_all | solution.py:64
  255.7 0.2 reduce_sum.12
  255.9 0.9 copy.41
  256.8 0.0 reduce-scatter.2.cloned.1.call-done
Async XLA Ops:
  7.2 44.8 %copy-start = (bf16[4096,256]{1,0:T(8,128)(2,1)S(1)}, bf16[4096,256]{1,0:T(8,128)(2,1)}, u32[]{:S(2)}) copy-start(bf16[4096,256]{1,0:T(8,128)(2,1)} %param.4) | copy-start | bytes 6291460
  9.3 29.0 %all-to-all-start = ((bf16[4,32,16,256]{3,2,1,0:T(8,128)(2,1)}), bf16[4,32,16,256]{3,2,1,0:T(8,128)(2,1)S(1)}, u32[]{:S(2)}, u32[]{:S(2)}) async-start(bf16[4,32,16,256]{3,2,1,0:T(8,128)(2,1)} %broadcast_in_dim.17), calls=%async_computation | async-start | bytes 2097152 | tf_op jit(solution)/shard_map/all_to_all | solution.py:44
  14.8 47.2 %all-gather.2.cloned.1.call-start = ((), (), s32[]{:S(2)}) async-start(), calls=%async_computation.5 | async-start | bytes 2359296 | tf_op jit(solution)/shard_map/all_gather | solution.py:83
  38.4 12.2 %collective-permute-start = (bf16[4,32,16,256]{3,2,1,0:T(8,128)(2,1)S(1)}, bf16[4,32,16,256]{3,2,1,0:T(8,128)(2,1)}, u32[]{:S(2)}, u32[]{:S(2)}) collective-permute-start(bf16[4,32,16,256]{3,2,1,0:T(8,128)(2,1)S(1)} %all-to-all-done), channel_id=1, source_target_pairs={{0,1},{1,0},{2,3},{3,2},{4,5},{5,4},{6,7},{7,6},{8,9},{9,8},{10,11... | collective-permute-start | bytes 3145736 | tf_op jit(solution)/shard_map/ppermute | solution.py:45
  135.6 2.3 copy-start.3
  135.6 3.0 %copy-start.4 = (bf16[4096,256]{1,0:T(8,128)(2,1)S(1)}, bf16[4096,256]{1,0:T(8,128)(2,1)}, u32[]{:S(2)}) copy-start(bf16[4096,256]{1,0:T(8,128)(2,1)} %param.5) | copy-start | bytes 6291460
  135.7 4.5 %copy-start.2 = (bf16[4,64,16,256]{3,2,1,0:T(8,128)(2,1)}, bf16[4,64,16,256]{3,2,1,0:T(8,128)(2,1)S(1)}, u32[]{:S(2)}) copy-start(bf16[4,64,16,256]{3,2,1,0:T(8,128)(2,1)S(1)} %copy.33) | copy-start | bytes 6291460
  140.3 1.4 copy-start.1
  143.2 64.9 %all-to-all-start.2 = ((bf16[4,64,16,256]{3,2,0,1:T(8,128)(2,1)}), bf16[4,64,16,256]{3,2,0,1:T(8,128)(2,1)}, u32[]{:S(2)}, u32[]{:S(2)}) async-start(bf16[4,64,16,256]{3,2,0,1:T(8,128)(2,1)} %copy.36), calls=%async_computation.2 | async-start | bytes 4194304 | tf_op jit(solution)/shard_map/all_to_all | solution.py:104
  150.7 106.1 %reduce-scatter.2.cloned.1.call-start = ((), (), s32[]{:S(2)}) async-start(), calls=%async_computation.6 | async-start | bytes 2359296 | tf_op jit(solution)/shard_map/reduce_scatter | solution.py:101
  212.6 12.1 %collective-permute-start.1 = (bf16[16,4,32,256]{3,2,0,1:T(8,128)(2,1)S(1)}, bf16[16,4,32,256]{3,2,0,1:T(8,128)(2,1)S(1)}, u32[]{:S(2)}, u32[]{:S(2)}) collective-permute-start(bf16[16,4,32,256]{3,2,0,1:T(8,128)(2,1)S(1)} %bitcast.64), channel_id=1, source_target_pairs={{0,1},{1,0},{2,3},{3,2},{4,5},{5,4},{6,7},{7,6},{8,9},{9,8},{10,11... | collective-permute-start | bytes 3145736 | tf_op jit(solution)/shard_map/ppermute | solution.py:61
Sparse Core Ops, SparseCore 0:
  17.7 44.2 all-gather.1
  159.9 61.8 reduce-scatter.1
